TPU v7x, 128 devices: a whole 4x4x4 slice. The times are simulated.
128 devices in a mesh: sta: 64 (over x_hi, y, z, core), day: 2 (over x_lo).
Axes of the slice: x: 4 (x_hi: 2, x_lo: 2; x = x_hi * 2 + x_lo), y: 4, z: 4, core: 2. Of those that a mesh axis runs over, the one named last changes fastest.
Arguments:
- spectra: bfloat16 [2, 12, 2, 3072, 640], P('day', None, None, 'sta'), as said below
- window_valid: int32 [2, 12], replicated, may hold values 0 or 1
- owner_order: int32 [4], replicated, may hold values from 0 to 63
Outputs:
- correlations: bfloat16 [4, 48, 3072, 256], P(None, 'day', 'sta')
Inputs may be any that keep to these rules, and one draw needn't show every extreme that they name: `spectra`: finite values.
All inputs are finite; a program needn't handle non-finite values.
Results may differ from a plain program's by a relative error of at most 0.0073.
Values may be sent and summed in bfloat16 or wider, within the bound.
No kernel may reach another device: no remote copies, remote signals or barrier semaphores. Data moves between devices by JAX's collectives and lax.ppermute only.
A program may use at most 192 MiB of HBM per device.

v0:
```python
import math

import jax
import jax.numpy as jnp
from jax import lax
from jax.sharding import PartitionSpec as P

STEPS = 4
LAGS = 256
NFFT = 2400
FIRST_BIN = 60

PART_ORDERS = (
    ((0, 1, 3, 5, 2), 4),
    ((0, 3, 5, 1, 4), 2),
    ((0, 5, 1, 3, 2), 4),
)


def swap(value, bit, size):
    return lax.ppermute(value, "sta", [(i, i ^ (1 << bit)) for i in range(size)])


def halve(buf, order, me, size):
    for bit in order:
        v = (me >> bit) & 1
        keep = lax.dynamic_index_in_dim(buf, v, 0, keepdims=False)
        send = lax.dynamic_index_in_dim(buf, 1 - v, 0, keepdims=False)
        buf = keep + swap(send, bit, size)
    return buf


def double(piece, order, me, size):
    buf = piece
    for bit in reversed(order):
        v = (me >> bit) & 1
        other = swap(buf, bit, size)
        lo = jnp.where(v == 1, other, buf)
        hi = jnp.where(v == 1, buf, other)
        buf = jnp.stack([lo, hi], axis=0)
    return buf


def broadcast_blocks(whitened, owner_order):
    size = lax.axis_size("sta")
    me = lax.axis_index("sta")
    masked = jnp.stack(
        [jnp.where(me == owner_order[s], whitened, jnp.zeros_like(whitened)) for s in range(STEPS)]
    )
    shape = masked.shape
    planes = masked.reshape((-1,) + shape[-2:])
    parts = len(PART_ORDERS)
    per_part = planes.shape[0] // parts
    outs = []
    for p, (order, exch) in enumerate(PART_ORDERS):
        buf = planes[p * per_part:(p + 1) * per_part]
        buf = buf.reshape((2,) * len(order) + (-1,) + shape[-2:])
        piece = halve(buf, order, me, size)
        piece = piece + swap(piece, exch, size)
        full = double(piece, order, me, size)
        outs.append(full.reshape((per_part,) + shape[-2:]))
    return jnp.concatenate(outs, axis=0).reshape(shape)


def whiten(spectra):
    values = spectra.astype(jnp.float32)
    energy = jnp.mean(values * values, axis=(2, 4), keepdims=True)
    return (values / jnp.sqrt(energy + 1e-06)).astype(jnp.bfloat16)


def lag_table(bins, lag_count):
    freq_index = FIRST_BIN + lax.iota(jnp.int32, bins)
    lag_index = lax.iota(jnp.int32, lag_count) - lag_count // 2
    phase = freq_index[:, None] * lag_index[None, :] % NFFT
    angle = phase.astype(jnp.float32) * (2.0 * math.pi / NFFT)
    return jnp.stack([jnp.cos(angle), -jnp.sin(angle)]).astype(jnp.bfloat16)


def day_correlation(owner, local, day_valid, lag_grid, stack_scale):
    masked = owner * day_valid.astype(jnp.bfloat16)[:, None, None, None]
    turned = jnp.concatenate([masked[:, 1:2], -masked[:, 0:1]], axis=1)
    wide = local.astype(jnp.float32)[:, :, None, :, :]
    real = jnp.sum(masked.astype(jnp.float32)[:, :, :, None, :] * wide, axis=(0, 1))
    imag = jnp.sum(turned.astype(jnp.float32)[:, :, :, None, :] * wide, axis=(0, 1))
    cross = jnp.concatenate([real, imag], axis=-1)
    cross = (cross * stack_scale).astype(jnp.bfloat16)
    a, b, kf = cross.shape
    lag_sums = jnp.dot(
        cross.reshape(a * b, kf), lag_grid.reshape(kf, -1), preferred_element_type=jnp.float32
    ).reshape(a, b, -1)
    return lag_sums * (1.0 / math.sqrt(kf // 2))


def body(spectra, window_valid, owner_order):
    day_index = lax.axis_index("day")
    whitened = whiten(spectra)[0]
    lag_grid = lag_table(whitened.shape[3], LAGS)
    stack_scale = 1.0 / math.sqrt(lax.axis_size("day") * whitened.shape[0])
    own_valid = lax.dynamic_index_in_dim(window_valid, day_index, 0, keepdims=False)
    owners = broadcast_blocks(whitened, owner_order)
    results = []
    for step_index in range(STEPS):
        lag_sums = day_correlation(owners[step_index], whitened, own_valid, lag_grid, stack_scale)
        share = lax.psum_scatter(
            lag_sums.astype(jnp.bfloat16), "day", scatter_dimension=0, tiled=True
        )
        results.append(share)
    return jnp.stack(results)


def solution(mesh):
    return jax.shard_map(
        body,
        mesh=mesh,
        in_specs=(P("day", None, None, "sta", None), P(), P()),
        out_specs=P(None, "day", "sta", None),
        check_vma=False,
    )
```

profile of v0, /device:TPU:1, one launch (start us, length us, event | category | flops | bytes accessed | tf_op | source)
XLA Modules:
  0.0 405.6 jit_solution(14060068045091838483)
XLA Ops:
  6.5 1.5 fusion.55
  10.4 1.7 fusion.12
  12.2 2.2 broadcast_select_fusion.3
  14.4 0.9 pad_maximum_fusion
  15.3 2.4 fusion.49
  17.8 2.4 dynamic-slice_bitcast_fusion.2
  20.1 1.4 collective-permute-start
  21.5 2.2 dynamic-slice_bitcast_fusion.1
  23.8 1.0 dynamic-slice_bitcast_fusion
  25.3 1.9 bitcast_convert_fusion
  27.2 3.1 cosine_convert_fusion
  30.4 1.4 bitcast_add_fusion.2
  31.8 1.8 collective-permute-start.1
  33.6 1.4 bitcast_add_fusion.1
  35.0 1.4 collective-permute-start.12
  36.4 1.3 bitcast_add_fusion
  37.8 2.8 collective-permute-start.23
  40.6 4.6 %collective-permute-done.1 = bf16[2,2,2,1,48,640]{5,4,2,1,0,3:T(8,128)(2,1)S(1)} collective-permute-done((bf16[2,2,2,1,48,640]{5,4,2,1,0,3:T(8,128)(2,1)S(1)}, bf16[2,2,2,1,48,640]{5,4,2,1,0,3:T(8,128)(2,1)S(1)}, u32[]{:S(2)}, u32[]{:S(2)}) %collective-permute-start.1) | collective-permute-done | bytes 491552 | tf_op jit(solution)/shard_map/ppermute | solution.py:21
  45.3 1.3 collective-permute-start.2
  46.6 1.0 collective-permute-done.12
  47.7 2.8 collective-permute-start.13
  50.5 1.1 collective-permute-done.23
  52.0 0.8 collective-permute-done.2
  52.9 2.8 collective-permute-start.3
  55.7 0.9 collective-permute-done.13
  57.9 1.7 collective-permute-done.3
  59.6 3.3 collective-permute-start.4
  63.0 2.5 collective-permute-start.15
  65.5 1.4 collective-permute-start.26
  67.0 0.7 collective-permute-start.5
  67.7 2.4 collective-permute-start.16
  70.2 1.6 collective-permute-start.27
  71.8 1.5 collective-permute-start.6
  73.3 0.9 pad_maximum_fusion.10
  74.3 2.0 collective-permute-start.17
  76.3 1.1 collective-permute-start.28
  77.5 3.0 collective-permute-start.7
  81.3 1.5 collective-permute-done.7
  83.0 2.1 collective-permute-done.18
  85.2 0.9 collective-permute-start.19
  86.9 1.5 collective-permute-done.8
  88.5 0.8 collective-permute-start.9
  89.3 2.6 collective-permute-done.19
  92.7 5.5 %collective-permute-done.9 = bf16[2,2,2,1,48,640]{5,4,2,1,0,3:T(8,128)(2,1)S(1)} collective-permute-done((bf16[2,2,2,1,48,640]{5,4,2,1,0,3:T(8,128)(2,1)S(1)}, bf16[2,2,2,1,48,640]{5,4,2,1,0,3:T(8,128)(2,1)S(1)}, u32[]{:S(2)}, u32[]{:S(2)}) %collective-permute-start.9) | collective-permute-done | bytes 491552 | tf_op jit(solution)/shard_map/ppermute | solution.py:21
  98.5 8.8 %collective-permute-start.10 = (bf16[2,2,2,2,1,48,640]{6,5,3,2,1,0,4:T(8,128)(2,1)S(1)}, bf16[2,2,2,2,1,48,640]{6,5,3,2,1,0,4:T(8,128)(2,1)S(1)}, u32[]{:S(2)}, u32[]{:S(2)}) collective-permute-start(bf16[2,2,2,2,1,48,640]{6,5,3,2,1,0,4:T(8,128)(2,1)S(1)} %fusion.28), channel_id=1, source_target_pairs={{0,2},{2,0},{4,6},{6,4},{8,10},{10,8},{12,14},{14,12},{16,18},{18,... | collective-permute-start | bytes 2949128 | tf_op jit(solution)/shard_map/ppermute | solution.py:21
  107.3 4.9 %collective-permute-start.31 = (bf16[2,2,2,1,48,640]{5,4,2,1,0,3:T(8,128)(2,1)S(1)}, bf16[2,2,2,1,48,640]{5,4,2,1,0,3:T(8,128)(2,1)S(1)}, u32[]{:S(2)}, u32[]{:S(2)}) collective-permute-start(bf16[2,2,2,1,48,640]{5,4,2,1,0,3:T(8,128)(2,1)S(1)} %pad_maximum_fusion.13), channel_id=1, source_target_pairs={{0,64},{2,66},{4,68},{6,70},{8,72},{10,74},{12,76},{14,78},{16,80}... | collective-permute-start | bytes 1474568 | tf_op jit(solution)/shard_map/ppermute | solution.py:21
  112.9 10.9 %collective-permute-done.31 = bf16[2,2,2,1,48,640]{5,4,2,1,0,3:T(8,128)(2,1)S(1)} collective-permute-done((bf16[2,2,2,1,48,640]{5,4,2,1,0,3:T(8,128)(2,1)S(1)}, bf16[2,2,2,1,48,640]{5,4,2,1,0,3:T(8,128)(2,1)S(1)}, u32[]{:S(2)}, u32[]{:S(2)}) %collective-permute-start.31) | collective-permute-done | bytes 491552 | tf_op jit(solution)/shard_map/ppermute | solution.py:21
  125.6 1.3 collective-permute-done.32
  127.9 5.6 %fusion.45 = (f32[12,2,48,640]{3,2,1,0:T(8,128)S(1)}, bf16[12,2,48,640]{3,2,1,0:T(8,128)(2,1)}, f32[12,2,48,640]{3,2,1,0:T(8,128)}, bf16[12,2,48,640]{3,2,1,0:T(...) fusion(bf16[12,2,48,640]{3,2,1,0:T(8,128)(2,1)S(1)} %bitcast.22, ...), kind=kLoop, calls=%fused_computation.156 | loop fusion | flops 5898240 | bytes 23592984 | tf_op jit(solution)/shard_map/convert_element_type | solution.py:83
  133.5 2.0 fusion.51
  135.5 1.8 maximum_convert_fusion.3
  137.3 1.7 maximum_convert_fusion.2
  139.3 0.9 copy-done.4
  140.5 1.8 maximum_convert_fusion.1
  142.3 1.8 maximum_convert_fusion
  144.0 138.9 %multiply_reduce_fusion.7 = (f32[48,48,640]{2,1,0:T(8,128)}, f32[48,48,640]{2,1,0:T(8,128)}, f32[48,48,640]{2,1,0:T(8,128)}, f32[48,48,640]{2,1,0:T(8,128)}, f32...) fusion(f32[12,2,48,640]{3,2,1,0:T(8,128)} %bitcast_convert_fusion, ...), kind=kLoop, calls=%fused_computation.7 | loop fusion | flops 554434560 | bytes 73728000 | tf_op jit(solution)/shard_map/reduce_sum | solution.py:83
  283.0 7.3 %multiply_convert_fusion.3 = bf16[48,48,256]{2,1,0:T(8,128)(2,1)} fusion(bf16[1280,256,1]{1,0,2:T(8,128)(2,1)} %bitcast.227, f32[48,48,640]{2,1,0:T(8,128)} %get-tuple-element.6, f32[48,48,640]{2,1,0:T(8,128)} %get-tuple-element.5), kind=kOutput, calls=%fused_computation.29 | convolution fusion | flops 1519976448 | bytes 13631488 | tf_op jit(solution)/shard_map/dot_general | solution.py:88
  290.5 7.1 %multiply_convert_fusion.2 = bf16[48,48,256]{2,1,0:T(8,128)(2,1)} fusion(bf16[1280,256,1]{1,0,2:T(8,128)(2,1)S(1)} %bitcast.228, f32[48,48,640]{2,1,0:T(8,128)} %get-tuple-element.8, f32[48,48,640]{2,1,0:T(8,128)} %get-tuple-element.7), kind=kOutput, calls=%fused_computation.28 | convolution fusion | flops 1519976448 | bytes 13631488 | tf_op jit(solution)/shard_map/dot_general | solution.py:88
  297.7 7.1 %multiply_convert_fusion.1 = bf16[48,48,256]{2,1,0:T(8,128)(2,1)} fusion(bf16[1280,256,1]{1,0,2:T(8,128)(2,1)S(1)} %bitcast.229, f32[48,48,640]{2,1,0:T(8,128)} %get-tuple-element.10, f32[48,48,640]{2,1,0:T(8,128)} %get-tuple-element.9), kind=kOutput, calls=%fused_computation.27 | convolution fusion | flops 1519976448 | bytes 13631488 | tf_op jit(solution)/shard_map/dot_general | solution.py:88
  305.0 7.2 %multiply_convert_fusion = bf16[48,48,256]{2,1,0:T(8,128)(2,1)} fusion(bf16[1280,256,1]{1,0,2:T(8,128)(2,1)S(1)} %bitcast.230, f32[48,48,640]{2,1,0:T(8,128)} %get-tuple-element.12, f32[48,48,640]{2,1,0:T(8,128)} %get-tuple-element.11), kind=kOutput, calls=%fused_computation.26 | convolution fusion | flops 1519976448 | bytes 13631488 | tf_op jit(solution)/shard_map/dot_general | solution.py:88
  312.8 27.7 %reduce-scatter.7.cloned.1.call-done = bf16[24,48,256]{2,1,0:T(8,128)(2,1)} async-done(((bf16[48,48,256]{2,1,0:T(8,128)(2,1)}), bf16[24,48,256]{2,1,0:T(8,128)(2,1)}) %reduce-scatter.7.cloned.1.call-update) | async-done | bytes 589840 | tf_op jit(solution)/shard_map/reduce_scatter | solution.py:104
  340.5 27.7 %reduce-scatter.9.cloned.1.call-done = bf16[24,48,256]{2,1,0:T(8,128)(2,1)} async-done(((bf16[48,48,256]{2,1,0:T(8,128)(2,1)}), bf16[24,48,256]{2,1,0:T(8,128)(2,1)}) %reduce-scatter.9.cloned.1.call-update) | async-done | bytes 589840 | tf_op jit(solution)/shard_map/reduce_scatter | solution.py:104
  368.2 27.6 %reduce-scatter.11.cloned.1.call-done = bf16[24,48,256]{2,1,0:T(8,128)(2,1)} async-done(((bf16[48,48,256]{2,1,0:T(8,128)(2,1)}), bf16[24,48,256]{2,1,0:T(8,128)(2,1)}) %reduce-scatter.11.cloned.1.call-update) | async-done | bytes 589840 | tf_op jit(solution)/shard_map/reduce_scatter | solution.py:104
  395.7 3.3 pad_maximum_fusion.1
  (121 shorter events, 10.7 us)
Async XLA Ops:
  6.5 306.3 %reduce-scatter.5.cloned.1.call-start = ((), (), s32[]{:S(2)}) async-start(), calls=%async_computation.4 | async-start | bytes 1769472 | tf_op jit(solution)/shard_map/reduce_scatter | solution.py:104
  17.8 7.5 %copy-start = (bf16[1,12,2,48,640]{4,3,2,1,0:T(8,128)(2,1)S(1)}, bf16[1,12,2,48,640]{4,3,2,1,0:T(8,128)(2,1)}, u32[]{:S(2)}) copy-start(bf16[1,12,2,48,640]{4,3,2,1,0:T(8,128)(2,1)} %param.3) | copy-start | bytes 4423684
  20.1 10.2 %collective-permute-start = (bf16[2,2,2,2,1,48,640]{6,5,3,2,1,0,4:T(8,128)(2,1)}, bf16[2,2,2,2,1,48,640]{6,5,3,2,1,0,4:T(8,128)(2,1)}, u32[]{:S(2)}, u32[]{:S(2)}) collective-permute-start(bf16[2,2,2,2,1,48,640]{6,5,3,2,1,0,4:T(8,128)(2,1)} %dynamic-slice_bitcast_fusion.2), channel_id=1, source_target_pairs={{0,2},{2,0},{4,6},{6,4},{8,10},{10,8},{12,14},{14,12},{16,18},{18,... | collective-permute-start | bytes 2949128 | tf_op jit(solution)/shard_map/ppermute | solution.py:21
  23.8 9.9 %collective-permute-start.11 = (bf16[2,2,2,2,1,48,640]{6,5,3,2,1,0,4:T(8,128)(2,1)}, bf16[2,2,2,2,1,48,640]{6,5,3,2,1,0,4:T(8,128)(2,1)}, u32[]{:S(2)}, u32[]{:S(2)}) collective-permute-start(bf16[2,2,2,2,1,48,640]{6,5,3,2,1,0,4:T(8,128)(2,1)} %dynamic-slice_bitcast_fusion.1), channel_id=1, source_target_pairs={{0,2},{2,0},{4,6},{6,4},{8,10},{10,8},{12,14},{14,12},{16,18},{18,... | collective-permute-start | bytes 2949128 | tf_op jit(solution)/shard_map/ppermute | solution.py:21
  24.8 11.6 %collective-permute-start.22 = (bf16[2,2,2,2,1,48,640]{6,5,3,2,1,0,4:T(8,128)(2,1)}, bf16[2,2,2,2,1,48,640]{6,5,3,2,1,0,4:T(8,128)(2,1)}, u32[]{:S(2)}, u32[]{:S(2)}) collective-permute-start(bf16[2,2,2,2,1,48,640]{6,5,3,2,1,0,4:T(8,128)(2,1)} %dynamic-slice_bitcast_fusion), channel_id=1, source_target_pairs={{0,2},{2,0},{4,6},{6,4},{8,10},{10,8},{12,14},{14,12},{16,18},{18,... | collective-permute-start | bytes 2949128 | tf_op jit(solution)/shard_map/ppermute | solution.py:21
  25.3 5.1 %copy-start.2 = (bf16[32,48,640]{2,1,0:T(8,128)(2,1)S(1)}, bf16[32,48,640]{2,1,0:T(8,128)(2,1)}, u32[]{:S(2)}) copy-start(bf16[32,48,640]{2,1,0:T(8,128)(2,1)} %get-tuple-element.23) | copy-start | bytes 5898244
  27.2 6.4 %copy-start.1 = (bf16[32,48,640]{2,1,0:T(8,128)(2,1)S(1)}, bf16[32,48,640]{2,1,0:T(8,128)(2,1)}, u32[]{:S(2)}) copy-start(bf16[32,48,640]{2,1,0:T(8,128)(2,1)} %get-tuple-element.22) | copy-start | bytes 5898244
  31.8 13.4 %collective-permute-start.1 = (bf16[2,2,2,1,48,640]{5,4,2,1,0,3:T(8,128)(2,1)S(1)}, bf16[2,2,2,1,48,640]{5,4,2,1,0,3:T(8,128)(2,1)S(1)}, u32[]{:S(2)}, u32[]{:S(2)}) collective-permute-start(bf16[2,2,2,1,48,640]{5,4,2,1,0,3:T(8,128)(2,1)S(1)} %dynamic-slice_bitcast_fusion.5), channel_id=1, source_target_pairs={{0,4},{2,6},{4,0},{6,2},{8,12},{10,14},{12,8},{14,10},{16,20},{18,... | collective-permute-start | bytes 1474568 | tf_op jit(solution)/shard_map/ppermute | solution.py:21
  35.0 12.6 %collective-permute-start.12 = (bf16[2,2,2,1,48,640]{5,4,2,1,0,3:T(8,128)(2,1)S(1)}, bf16[2,2,2,1,48,640]{5,4,2,1,0,3:T(8,128)(2,1)S(1)}, u32[]{:S(2)}, u32[]{:S(2)}) collective-permute-start(bf16[2,2,2,1,48,640]{5,4,2,1,0,3:T(8,128)(2,1)S(1)} %dynamic-slice_bitcast_fusion.4), channel_id=1, source_target_pairs={{0,16},{2,18},{4,20},{6,22},{8,24},{10,26},{12,28},{14,30},{16,0},... | collective-permute-start | bytes 1474568 | tf_op jit(solution)/shard_map/ppermute | solution.py:21
  37.8 13.8 %collective-permute-start.23 = (bf16[2,2,2,1,48,640]{5,4,2,1,0,3:T(8,128)(2,1)S(1)}, bf16[2,2,2,1,48,640]{5,4,2,1,0,3:T(8,128)(2,1)S(1)}, u32[]{:S(2)}, u32[]{:S(2)}) collective-permute-start(bf16[2,2,2,1,48,640]{5,4,2,1,0,3:T(8,128)(2,1)S(1)} %dynamic-slice_bitcast_fusion.3), channel_id=1, source_target_pairs={{0,64},{2,66},{4,68},{6,70},{8,72},{10,74},{12,76},{14,78},{16,80}... | collective-permute-start | bytes 1474568 | tf_op jit(solution)/shard_map/ppermute | solution.py:21
  45.3 7.5 %collective-permute-start.2 = (bf16[2,2,1,48,640]{4,3,1,2,0:T(8,128)(2,1)S(1)}, bf16[2,2,1,48,640]{4,3,1,2,0:T(8,128)(2,1)S(1)}, u32[]{:S(2)}, u32[]{:S(2)}) collective-permute-start(bf16[2,2,1,48,640]{4,3,1,2,0:T(8,128)(2,1)S(1)} %dynamic-slice_bitcast_fusion.8), channel_id=1, source_target_pairs={{0,16},{2,18},{4,20},{6,22},{8,24},{10,26},{12,28},{14,30},{16,0},... | collective-permute-start | bytes 737288 | tf_op jit(solution)/shard_map/ppermute | solution.py:21
  47.7 8.9 %collective-permute-start.13 = (bf16[2,2,1,48,640]{4,3,1,2,0:T(8,128)(2,1)S(1)}, bf16[2,2,1,48,640]{4,3,1,2,0:T(8,128)(2,1)S(1)}, u32[]{:S(2)}, u32[]{:S(2)}) collective-permute-start(bf16[2,2,1,48,640]{4,3,1,2,0:T(8,128)(2,1)S(1)} %dynamic-slice_bitcast_fusion.7), channel_id=1, source_target_pairs={{0,64},{2,66},{4,68},{6,70},{8,72},{10,74},{12,76},{14,78},{16,80}... | collective-permute-start | bytes 737288 | tf_op jit(solution)/shard_map/ppermute | solution.py:21
  51.7 5.6 %collective-permute-start.24 = (bf16[2,2,1,48,640]{4,3,1,2,0:T(8,128)(2,1)S(1)}, bf16[2,2,1,48,640]{4,3,1,2,0:T(8,128)(2,1)S(1)}, u32[]{:S(2)}, u32[]{:S(2)}) collective-permute-start(bf16[2,2,1,48,640]{4,3,1,2,0:T(8,128)(2,1)S(1)} %dynamic-slice_bitcast_fusion.6), channel_id=1, source_target_pairs={{0,4},{2,6},{4,0},{6,2},{8,12},{10,14},{12,8},{14,10},{16,20},{18,... | collective-permute-start | bytes 737288 | tf_op jit(solution)/shard_map/ppermute | solution.py:21
  52.9 6.7 %collective-permute-start.3 = (bf16[2,1,48,640]{3,2,1,0:T(8,128)(2,1)S(1)}, bf16[2,1,48,640]{3,2,1,0:T(8,128)(2,1)S(1)}, u32[]{:S(2)}, u32[]{:S(2)}) collective-permute-start(bf16[2,1,48,640]{3,2,1,0:T(8,128)(2,1)S(1)} %dynamic-slice_bitcast_fusion.11), channel_id=1, source_target_pairs={{0,64},{2,66},{4,68},{6,70},{8,72},{10,74},{12,76},{14,78},{16,80}... | collective-permute-start | bytes 368648 | tf_op jit(solution)/shard_map/ppermute | solution.py:21
  56.7 6.2 %collective-permute-start.14 = (bf16[2,1,48,640]{3,2,1,0:T(8,128)(2,1)S(1)}, bf16[2,1,48,640]{3,2,1,0:T(8,128)(2,1)S(1)}, u32[]{:S(2)}, u32[]{:S(2)}) collective-permute-start(bf16[2,1,48,640]{3,2,1,0:T(8,128)(2,1)S(1)} %dynamic-slice_bitcast_fusion.10), channel_id=1, source_target_pairs={{0,4},{2,6},{4,0},{6,2},{8,12},{10,14},{12,8},{14,10},{16,20},{18,... | collective-permute-start | bytes 368648 | tf_op jit(solution)/shard_map/ppermute | solution.py:21
  57.3 8.1 %collective-permute-start.25 = (bf16[2,1,48,640]{3,2,1,0:T(8,128)(2,1)S(1)}, bf16[2,1,48,640]{3,2,1,0:T(8,128)(2,1)S(1)}, u32[]{:S(2)}, u32[]{:S(2)}) collective-permute-start(bf16[2,1,48,640]{3,2,1,0:T(8,128)(2,1)S(1)} %dynamic-slice_bitcast_fusion.9), channel_id=1, source_target_pairs={{0,16},{2,18},{4,20},{6,22},{8,24},{10,26},{12,28},{14,30},{16,0},... | collective-permute-start | bytes 368648 | tf_op jit(solution)/shard_map/ppermute | solution.py:21
  59.6 7.3 %collective-permute-start.4 = (bf16[1,48,640]{2,1,0:T(8,128)(2,1)S(1)}, bf16[1,48,640]{2,1,0:T(8,128)(2,1)S(1)}, u32[]{:S(2)}, u32[]{:S(2)}) collective-permute-start(bf16[1,48,640]{2,1,0:T(8,128)(2,1)S(1)} %dynamic-slice_bitcast_fusion.14), channel_id=1, source_target_pairs={{0,8},{2,10},{4,12},{6,14},{8,0},{10,2},{12,4},{14,6},{16,24},{18,... | collective-permute-start | bytes 184328 | tf_op jit(solution)/shard_map/ppermute | solution.py:21
  63.0 4.7 %collective-permute-start.15 = (bf16[1,48,640]{2,1,0:T(8,128)(2,1)S(1)}, bf16[1,48,640]{2,1,0:T(8,128)(2,1)S(1)}, u32[]{:S(2)}, u32[]{:S(2)}) collective-permute-start(bf16[1,48,640]{2,1,0:T(8,128)(2,1)S(1)} %dynamic-slice_bitcast_fusion.13), channel_id=1, source_target_pairs={{0,32},{2,34},{4,36},{6,38},{8,40},{10,42},{12,44},{14,46},{16,48}... | collective-permute-start | bytes 184328 | tf_op jit(solution)/shard_map/ppermute | solution.py:21
  65.5 4.7 %collective-permute-start.26 = (bf16[1,48,640]{2,1,0:T(8,128)(2,1)S(1)}, bf16[1,48,640]{2,1,0:T(8,128)(2,1)S(1)}, u32[]{:S(2)}, u32[]{:S(2)}) collective-permute-start(bf16[1,48,640]{2,1,0:T(8,128)(2,1)S(1)} %dynamic-slice_bitcast_fusion.12), channel_id=1, source_target_pairs={{0,8},{2,10},{4,12},{6,14},{8,0},{10,2},{12,4},{14,6},{16,24},{18,... | collective-permute-start | bytes 184328 | tf_op jit(solution)/shard_map/ppermute | solution.py:21
  67.0 4.9 %collective-permute-start.5 = (bf16[1,48,640]{2,1,0:T(8,128)(2,1)S(1)}, bf16[1,48,640]{2,1,0:T(8,128)(2,1)S(1)}, u32[]{:S(2)}, u32[]{:S(2)}) collective-permute-start(bf16[1,48,640]{2,1,0:T(8,128)(2,1)S(1)} %bitcast_add_fusion.14), channel_id=1, source_target_pairs={{0,32},{2,34},{4,36},{6,38},{8,40},{10,42},{12,44},{14,46},{16,48}... | collective-permute-start | bytes 184328 | tf_op jit(solution)/shard_map/ppermute | solution.py:21
  67.7 6.5 %collective-permute-start.16 = (bf16[1,48,640]{2,1,0:T(8,128)(2,1)S(1)}, bf16[1,48,640]{2,1,0:T(8,128)(2,1)S(1)}, u32[]{:S(2)}, u32[]{:S(2)}) collective-permute-start(bf16[1,48,640]{2,1,0:T(8,128)(2,1)S(1)} %bitcast_add_fusion.13), channel_id=1, source_target_pairs={{0,8},{2,10},{4,12},{6,14},{8,0},{10,2},{12,4},{14,6},{16,24},{18,... | collective-permute-start | bytes 184328 | tf_op jit(solution)/shard_map/ppermute | solution.py:21
  70.2 6.1 %collective-permute-start.27 = (bf16[1,48,640]{2,1,0:T(8,128)(2,1)S(1)}, bf16[1,48,640]{2,1,0:T(8,128)(2,1)S(1)}, u32[]{:S(2)}, u32[]{:S(2)}) collective-permute-start(bf16[1,48,640]{2,1,0:T(8,128)(2,1)S(1)} %bitcast_add_fusion.12), channel_id=1, source_target_pairs={{0,32},{2,34},{4,36},{6,38},{8,40},{10,42},{12,44},{14,46},{16,48}... | collective-permute-start | bytes 184328 | tf_op jit(solution)/shard_map/ppermute | solution.py:21
  71.8 5.6 %collective-permute-start.6 = (bf16[1,48,640]{2,1,0:T(8,128)(2,1)S(1)}, bf16[1,48,640]{2,1,0:T(8,128)(2,1)S(1)}, u32[]{:S(2)}, u32[]{:S(2)}) collective-permute-start(bf16[1,48,640]{2,1,0:T(8,128)(2,1)S(1)} %add.195), channel_id=1, source_target_pairs={{0,8},{2,10},{4,12},{6,14},{8,0},{10,2},{12,4},{14,6},{16,24},{18,... | collective-permute-start | bytes 184328 | tf_op jit(solution)/shard_map/ppermute | solution.py:21
  74.3 6.3 %collective-permute-start.17 = (bf16[1,48,640]{2,1,0:T(8,128)(2,1)S(1)}, bf16[1,48,640]{2,1,0:T(8,128)(2,1)S(1)}, u32[]{:S(2)}, u32[]{:S(2)}) collective-permute-start(bf16[1,48,640]{2,1,0:T(8,128)(2,1)S(1)} %add.207), channel_id=1, source_target_pairs={{0,32},{2,34},{4,36},{6,38},{8,40},{10,42},{12,44},{14,46},{16,48}... | collective-permute-start | bytes 184328 | tf_op jit(solution)/shard_map/ppermute | solution.py:21
  76.3 4.7 %collective-permute-start.28 = (bf16[1,48,640]{2,1,0:T(8,128)(2,1)S(1)}, bf16[1,48,640]{2,1,0:T(8,128)(2,1)S(1)}, u32[]{:S(2)}, u32[]{:S(2)}) collective-permute-start(bf16[1,48,640]{2,1,0:T(8,128)(2,1)S(1)} %add.213), channel_id=1, source_target_pairs={{0,8},{2,10},{4,12},{6,14},{8,0},{10,2},{12,4},{14,6},{16,24},{18,... | collective-permute-start | bytes 184328 | tf_op jit(solution)/shard_map/ppermute | solution.py:21
  77.5 5.3 %collective-permute-start.7 = (bf16[2,1,48,640]{3,2,0,1:T(8,128)(2,1)S(1)}, bf16[2,1,48,640]{3,2,0,1:T(8,128)(2,1)S(1)}, u32[]{:S(2)}, u32[]{:S(2)}) collective-permute-start(bf16[2,1,48,640]{3,2,0,1:T(8,128)(2,1)S(1)} %fusion.34), channel_id=1, source_target_pairs={{0,64},{2,66},{4,68},{6,70},{8,72},{10,74},{12,76},{14,78},{16,80}... | collective-permute-start | bytes 368648 | tf_op jit(solution)/shard_map/ppermute | solution.py:21
  80.6 4.6 %collective-permute-start.18 = (bf16[2,1,48,640]{3,2,0,1:T(8,128)(2,1)S(1)}, bf16[2,1,48,640]{3,2,0,1:T(8,128)(2,1)S(1)}, u32[]{:S(2)}, u32[]{:S(2)}) collective-permute-start(bf16[2,1,48,640]{3,2,0,1:T(8,128)(2,1)S(1)} %pad_maximum_fusion.18), channel_id=1, source_target_pairs={{0,4},{2,6},{4,0},{6,2},{8,12},{10,14},{12,8},{14,10},{16,20},{18,... | collective-permute-start | bytes 368648 | tf_op jit(solution)/shard_map/ppermute | solution.py:21
  81.0 5.1 %collective-permute-start.29 = (bf16[2,1,48,640]{3,2,0,1:T(8,128)(2,1)S(1)}, bf16[2,1,48,640]{3,2,0,1:T(8,128)(2,1)S(1)}, u32[]{:S(2)}, u32[]{:S(2)}) collective-permute-start(bf16[2,1,48,640]{3,2,0,1:T(8,128)(2,1)S(1)} %pad_maximum_fusion.19), channel_id=1, source_target_pairs={{0,16},{2,18},{4,20},{6,22},{8,24},{10,26},{12,28},{14,30},{16,0},... | collective-permute-start | bytes 368648 | tf_op jit(solution)/shard_map/ppermute | solution.py:21
  82.9 5.4 %collective-permute-start.8 = (bf16[2,2,1,48,640]{4,3,1,0,2:T(8,128)(2,1)S(1)}, bf16[2,2,1,48,640]{4,3,1,0,2:T(8,128)(2,1)S(1)}, u32[]{:S(2)}, u32[]{:S(2)}) collective-permute-start(bf16[2,2,1,48,640]{4,3,1,0,2:T(8,128)(2,1)S(1)} %fusion.32), channel_id=1, source_target_pairs={{0,16},{2,18},{4,20},{6,22},{8,24},{10,26},{12,28},{14,30},{16,0},... | collective-permute-start | bytes 737288 | tf_op jit(solution)/shard_map/ppermute | solution.py:21
  85.2 6.6 %collective-permute-start.19 = (bf16[2,2,1,48,640]{4,3,1,0,2:T(8,128)(2,1)S(1)}, bf16[2,2,1,48,640]{4,3,1,0,2:T(8,128)(2,1)S(1)}, u32[]{:S(2)}, u32[]{:S(2)}) collective-permute-start(bf16[2,2,1,48,640]{4,3,1,0,2:T(8,128)(2,1)S(1)} %pad_maximum_fusion.15), channel_id=1, source_target_pairs={{0,64},{2,66},{4,68},{6,70},{8,72},{10,74},{12,76},{14,78},{16,80}... | collective-permute-start | bytes 737288 | tf_op jit(solution)/shard_map/ppermute | solution.py:21
  86.2 6.4 %collective-permute-start.30 = (bf16[2,2,1,48,640]{4,3,1,0,2:T(8,128)(2,1)S(1)}, bf16[2,2,1,48,640]{4,3,1,0,2:T(8,128)(2,1)S(1)}, u32[]{:S(2)}, u32[]{:S(2)}) collective-permute-start(bf16[2,2,1,48,640]{4,3,1,0,2:T(8,128)(2,1)S(1)} %pad_maximum_fusion.16), channel_id=1, source_target_pairs={{0,4},{2,6},{4,0},{6,2},{8,12},{10,14},{12,8},{14,10},{16,20},{18,... | collective-permute-start | bytes 737288 | tf_op jit(solution)/shard_map/ppermute | solution.py:21
  88.5 9.7 %collective-permute-start.9 = (bf16[2,2,2,1,48,640]{5,4,2,1,0,3:T(8,128)(2,1)S(1)}, bf16[2,2,2,1,48,640]{5,4,2,1,0,3:T(8,128)(2,1)S(1)}, u32[]{:S(2)}, u32[]{:S(2)}) collective-permute-start(bf16[2,2,2,1,48,640]{5,4,2,1,0,3:T(8,128)(2,1)S(1)} %fusion.30), channel_id=1, source_target_pairs={{0,4},{2,6},{4,0},{6,2},{8,12},{10,14},{12,8},{14,10},{16,20},{18,... | collective-permute-start | bytes 1474568 | tf_op jit(solution)/shard_map/ppermute | solution.py:21
  92.0 20.2 %collective-permute-start.20 = (bf16[2,2,2,1,48,640]{5,4,2,1,0,3:T(8,128)(2,1)S(1)}, bf16[2,2,2,1,48,640]{5,4,2,1,0,3:T(8,128)(2,1)S(1)}, u32[]{:S(2)}, u32[]{:S(2)}) collective-permute-start(bf16[2,2,2,1,48,640]{5,4,2,1,0,3:T(8,128)(2,1)S(1)} %pad_maximum_fusion.12), channel_id=1, source_target_pairs={{0,16},{2,18},{4,20},{6,22},{8,24},{10,26},{12,28},{14,30},{16,0},... | collective-permute-start | bytes 1474568 | tf_op jit(solution)/shard_map/ppermute | solution.py:21
  92.7 19.5 %copy-start.6 = (s32[2,12]{1,0:T(2,128)S(1)}, s32[2,12]{1,0:T(2,128)}, u32[]{:S(2)}) copy-start(s32[2,12]{1,0:T(2,128)} %param.4) | copy-start | bytes 292
  98.5 26.2 %collective-permute-start.10 = (bf16[2,2,2,2,1,48,640]{6,5,3,2,1,0,4:T(8,128)(2,1)S(1)}, bf16[2,2,2,2,1,48,640]{6,5,3,2,1,0,4:T(8,128)(2,1)S(1)}, u32[]{:S(2)}, u32[]{:S(2)}) collective-permute-start(bf16[2,2,2,2,1,48,640]{6,5,3,2,1,0,4:T(8,128)(2,1)S(1)} %fusion.28), channel_id=1, source_target_pairs={{0,2},{2,0},{4,6},{6,4},{8,10},{10,8},{12,14},{14,12},{16,18},{18,... | collective-permute-start | bytes 2949128 | tf_op jit(solution)/shard_map/ppermute | solution.py:21
  107.3 16.5 %collective-permute-start.31 = (bf16[2,2,2,1,48,640]{5,4,2,1,0,3:T(8,128)(2,1)S(1)}, bf16[2,2,2,1,48,640]{5,4,2,1,0,3:T(8,128)(2,1)S(1)}, u32[]{:S(2)}, u32[]{:S(2)}) collective-permute-start(bf16[2,2,2,1,48,640]{5,4,2,1,0,3:T(8,128)(2,1)S(1)} %pad_maximum_fusion.13), channel_id=1, source_target_pairs={{0,64},{2,66},{4,68},{6,70},{8,72},{10,74},{12,76},{14,78},{16,80}... | collective-permute-start | bytes 1474568 | tf_op jit(solution)/shard_map/ppermute | solution.py:21
  112.5 12.7 %collective-permute-start.21 = (bf16[2,2,2,2,1,48,640]{6,5,3,2,1,0,4:T(8,128)(2,1)S(1)}, bf16[2,2,2,2,1,48,640]{6,5,3,2,1,0,4:T(8,128)(2,1)S(1)}, u32[]{:S(2)}, u32[]{:S(2)}) collective-permute-start(bf16[2,2,2,2,1,48,640]{6,5,3,2,1,0,4:T(8,128)(2,1)S(1)} %pad_maximum_fusion.8), channel_id=1, source_target_pairs={{0,2},{2,0},{4,6},{6,4},{8,10},{10,8},{12,14},{14,12},{16,18},{18,... | collective-permute-start | bytes 2949128 | tf_op jit(solution)/shard_map/ppermute | solution.py:21
  124.0 2.9 collective-permute-start.32
  137.3 1.9 copy-start.3
  137.3 2.9 copy-start.4
  283.0 7.6 %copy-start.5 = (bf16[2,640,256]{2,1,0:T(8,128)(2,1)S(1)}, bf16[2,640,256]{2,1,0:T(8,128)(2,1)}, u32[]{:S(2)}) copy-start(bf16[2,640,256]{2,1,0:T(8,128)(2,1)} %pad_maximum_fusion.10) | copy-start | bytes 1966084
  290.3 50.2 %reduce-scatter.7.cloned.1.call-start = ((), (), s32[]{:S(2)}) async-start(), calls=%async_computation.5 | async-start | bytes 1769472 | tf_op jit(solution)/shard_map/reduce_scatter | solution.py:104
  297.7 70.5 %reduce-scatter.9.cloned.1.call-start = ((), (), s32[]{:S(2)}) async-start(), calls=%async_computation.6 | async-start | bytes 1769472 | tf_op jit(solution)/shard_map/reduce_scatter | solution.py:104
  304.9 90.8 %reduce-scatter.11.cloned.1.call-start = ((), (), s32[]{:S(2)}) async-start(), calls=%async_computation.7 | async-start | bytes 1769472 | tf_op jit(solution)/shard_map/reduce_scatter | solution.py:104
Sparse Core Ops, SparseCore 0:
  290.4 22.3 reduce-scatter.4
  315.1 25.3 reduce-scatter.6
  342.8 25.3 reduce-scatter.8
  370.4 25.3 reduce-scatter.10
where the time goes:
time: 406 us
  other arithmetic  176 us (43%)
  waiting for transfers between devices  121 us (30%)
  starting transfers between devices  53.4 us (13%)
  matrix products  28.7 us (7%)
  between operations  16.1 us (4%)
  local copies, waits for them, and re-layouts  11.1 us (3%)
    reduce_sum x1, other arithmetic, day_correlation(): jnp.sum(masked.astype(jnp.float32)[:, :, :, None, :] * wide, axis=(0, 1))  139 us
    reduce_scatter x4, waiting for transfers between devices, body(): lax.psum_scatter(lag_sums.astype(jnp.bfloat16), 'day', scatter_dimension=...  83.6 us
    ppermute x33, starting transfers between devices, swap(): return lax.ppermute(value, 'sta', [(i, i ^ 1 << bit) for i in range(size)])  53.1 us
    ppermute x33, waiting for transfers between devices, swap(): return lax.ppermute(value, 'sta', [(i, i ^ 1 << bit) for i in range(size)])  37 us
    dot_general x4, matrix products, day_correlation(): jnp.dot(cross.reshape(a * b, kf), lag_grid.reshape(kf, -1), preferred_ele...  28.7 us
  transfers between devices with their start and end apart: 37, of which 21 were waited for; matrix products, arithmetic and copies ran while one was open for 9% of the time, Pallas kernels for 0%

commit v1 on v0

--- a/solution.py
+++ b/solution.py
@@ -99,8 +99,12 @@
     own_valid = lax.dynamic_index_in_dim(window_valid, day_index, 0, keepdims=False)
     owners = broadcast_blocks(whitened, owner_order)
     results = []
+    local = whitened
     for step_index in range(STEPS):
-        lag_sums = day_correlation(owners[step_index], whitened, own_valid, lag_grid, stack_scale)
+        if step_index >= 2:
+            local, results[step_index - 2] = lax.optimization_barrier((local, results[step_index - 2]))
+        lag_sums = day_correlation(owners[step_index], local, own_valid, lag_grid, stack_scale)
+        lag_sums, local = lax.optimization_barrier((lag_sums, local))
         share = lax.psum_scatter(
             lag_sums.astype(jnp.bfloat16), "day", scatter_dimension=0, tiled=True
         )

time: 406 us -> 372 us (0.916)
  waiting for transfers between devices: 121 us -> 80.2 us
  local copies, waits for them, and re-layouts: 11.1 us -> 16.2 us
  other arithmetic: 176 us -> 181 us
  starting transfers between devices: 53.4 us -> 48.5 us
    reduce_scatter x4, waiting for transfers between devices: 83.6 us -> 49.1 us  [body(): lax.psum_scatter(lag_sums.astype(jnp.bfloat16), 'day', scatter_dimension=...]
    ppermute x33, waiting for transfers between devices: 37 us -> 30.5 us  [swap(): return lax.ppermute(value, 'sta', [(i, i ^ 1 << bit) for i in range(size)])]
    ppermute x33, starting transfers between devices: 53.1 us -> 48.2 us  [swap(): return lax.ppermute(value, 'sta', [(i, i ^ 1 << bit) for i in range(size)])]
    unnamed x14 -> x32, local copies, waits for them, and re-layouts: 1.17 us -> 5.89 us
    reduce_sum x1 -> x4, other arithmetic: 139 us -> 139 us  [day_correlation(): jnp.sum(masked.astype(jnp.float32)[:, :, :, None, :] * wide, axis=(0, 1))]
  transfers between devices with their start and end apart: 37 -> 37, of which waited for: 21 -> 17; matrix products, arithmetic and copies ran while one was open for 9% -> 29% of each run, Pallas kernels for 0% -> 0%
where the time goes in v1:
time: 372 us; the launch traced here: 371 us
  other arithmetic  181 us (49%)
  waiting for transfers between devices  80.2 us (22%)
  starting transfers between devices  48.5 us (13%)
  matrix products  28.9 us (8%)
  local copies, waits for them, and re-layouts  16.2 us (4%)
  between operations  16.1 us (4%)
    reduce_sum x4, other arithmetic, day_correlation(): jnp.sum(masked.astype(jnp.float32)[:, :, :, None, :] * wide, axis=(0, 1))  139 us
    reduce_scatter x4, waiting for transfers between devices, body(): lax.psum_scatter(lag_sums.astype(jnp.bfloat16), 'day', scatter_dimension=...  49.1 us
    ppermute x33, starting transfers between devices, swap(): return lax.ppermute(value, 'sta', [(i, i ^ 1 << bit) for i in range(size)])  48.2 us
    ppermute x33, waiting for transfers between devices, swap(): return lax.ppermute(value, 'sta', [(i, i ^ 1 << bit) for i in range(size)])  30.5 us
    dot_general x4, matrix products, day_correlation(): jnp.dot(cross.reshape(a * b, kf), lag_grid.reshape(kf, -1), preferred_ele...  28.9 us
  transfers between devices with their start and end apart: 37, of which 17 were waited for; matrix products, arithmetic and copies ran while one was open for 29% of the time, Pallas kernels for 0%

profile of v1, /device:TPU:1, one launch (start us, length us, event | category | flops | bytes accessed | tf_op | source)
XLA Modules:
  0.0 370.8 jit_solution(14846590732141608789)
XLA Ops:
  6.5 1.7 fusion.12
  8.3 1.5 fusion.60
  12.1 2.2 broadcast_select_fusion.3
  15.3 2.8 fusion.54
  18.1 2.4 dynamic-slice_bitcast_fusion
  20.4 1.4 collective-permute-start.22
  21.8 2.3 dynamic-slice_bitcast_fusion.1
  24.1 1.0 dynamic-slice_bitcast_fusion.2
  25.7 2.1 fusion.49
  27.8 3.1 cosine_convert_fusion
  30.9 1.3 bitcast_add_fusion
  32.3 2.9 collective-permute-start.23
  35.3 1.4 bitcast_add_fusion.1
  36.7 1.4 collective-permute-start.12
  38.1 1.4 bitcast_add_fusion.2
  39.5 1.7 collective-permute-start.1
  41.2 5.5 %collective-permute-done.23 = bf16[2,2,2,1,48,640]{5,4,2,1,0,3:T(8,128)(2,1)S(1)} collective-permute-done((bf16[2,2,2,1,48,640]{5,4,2,1,0,3:T(8,128)(2,1)S(1)}, bf16[2,2,2,1,48,640]{5,4,2,1,0,3:T(8,128)(2,1)S(1)}, u32[]{:S(2)}, u32[]{:S(2)}) %collective-permute-start.23) | collective-permute-done | bytes 491552 | tf_op jit(solution)/shard_map/ppermute | solution.py:21
  46.8 1.8 collective-permute-start.24
  49.3 2.2 collective-permute-start.13
  53.0 4.4 %collective-permute-done.24 = bf16[2,2,1,48,640]{4,3,1,2,0:T(8,128)(2,1)S(1)} collective-permute-done((bf16[2,2,1,48,640]{4,3,1,2,0:T(8,128)(2,1)S(1)}, bf16[2,2,1,48,640]{4,3,1,2,0:T(8,128)(2,1)S(1)}, u32[]{:S(2)}, u32[]{:S(2)}) %collective-permute-start.24) | collective-permute-done | bytes 245792 | tf_op jit(solution)/shard_map/ppermute | solution.py:21
  57.7 1.4 collective-permute-start.14
  60.0 1.3 collective-permute-done.25
  61.3 3.6 collective-permute-start.26
  65.0 2.7 collective-permute-start.15
  68.3 2.6 collective-permute-start.27
  70.9 1.7 collective-permute-start.16
  72.7 1.4 collective-permute-start.5
  74.1 1.9 collective-permute-start.28
  76.9 1.3 collective-permute-start.17
  78.2 2.2 collective-permute-start.6
  80.5 1.5 collective-permute-done.17
  83.6 1.2 collective-permute-start.7
  85.0 1.2 collective-permute-done.18
  87.2 1.9 collective-permute-done.7
  90.3 3.0 collective-permute-start.31
  93.5 1.2 collective-permute-done.8
  94.9 9.6 %collective-permute-done.31 = bf16[2,2,2,1,48,640]{5,4,2,1,0,3:T(8,128)(2,1)S(1)} collective-permute-done((bf16[2,2,2,1,48,640]{5,4,2,1,0,3:T(8,128)(2,1)S(1)}, bf16[2,2,2,1,48,640]{5,4,2,1,0,3:T(8,128)(2,1)S(1)}, u32[]{:S(2)}, u32[]{:S(2)}) %collective-permute-start.31) | collective-permute-done | bytes 491552 | tf_op jit(solution)/shard_map/ppermute | solution.py:21
  104.7 4.8 %collective-permute-start.32 = (bf16[2,2,2,2,1,48,640]{6,5,3,2,1,0,4:T(8,128)(2,1)S(1)}, bf16[2,2,2,2,1,48,640]{6,5,3,2,1,0,4:T(8,128)(2,1)S(1)}, u32[]{:S(2)}, u32[]{:S(2)}) collective-permute-start(bf16[2,2,2,2,1,48,640]{6,5,3,2,1,0,4:T(8,128)(2,1)S(1)} %pad_maximum_fusion.9), channel_id=1, source_target_pairs={{0,2},{2,0},{4,6},{6,4},{8,10},{10,8},{12,14},{14,12},{16,18},{18,... | collective-permute-start | bytes 2949128 | tf_op jit(solution)/shard_map/ppermute | solution.py:21
  109.7 2.6 collective-permute-start.21
  112.5 1.3 collective-permute-start.10
  114.9 1.2 collective-permute-done.10
  116.6 1.4 fusion.55
  118.0 7.0 %fusion.50 = (f32[12,2,48,640]{3,2,1,0:T(8,128)}, bf16[12,2,48,640]{3,2,1,0:T(8,128)(2,1)}, f32[12,2,48,640]{3,2,1,0:T(8,128)S(1)}, bf16[12,2,48,640]{3,2,1,0:T(...) fusion(bf16[12,2,48,640]{3,2,1,0:T(8,128)(2,1)S(1)} %bitcast.22, ...), kind=kLoop, calls=%fused_computation.157 | loop fusion | flops 5898240 | bytes 23592984 | tf_op jit(solution)/shard_map/convert_element_type | solution.py:83
  125.0 2.0 fusion.58
  127.1 1.8 maximum_convert_fusion
  128.9 1.1 copy-done.4
  130.0 34.2 %multiply_reduce_fusion.7 = (f32[48,48,640]{2,1,0:T(8,128)}, f32[48,48,640]{2,1,0:T(8,128)}) fusion(f32[12,2,48,640]{3,2,1,0:T(8,128)S(1)} %copy-done.4, f32[12,2,48,640]{3,2,1,0:T(8,128)S(1)} %get-tuple-element.88, f32[12,2,48,640]{3,2,1,0:T(8,128)} %maximum_convert_fusion), kind=kLoop, calls=%fused_computation.7 | loop fusion | flops 138608640 | bytes 20643840 | tf_op jit(solution)/shard_map/reduce_sum | solution.py:83
  164.2 7.2 %fusion.14 = bf16[48,48,256]{2,1,0:T(8,128)(2,1)} fusion(bf16[1280,256,1]{1,0,2:T(8,128)(2,1)} %bitcast.227, f32[48,48,640]{2,1,0:T(8,128)} %get-tuple-element.34, f32[48,48,640]{2,1,0:T(8,128)} %get-tuple-element.33), kind=kOutput, calls=%fused_computation.30 | convolution fusion | flops 1519976448 | bytes 13631488 | tf_op jit(solution)/shard_map/dot_general | solution.py:88
  171.4 1.9 convert_element_type.155
  173.8 1.6 copy-done.3
  175.4 36.0 %multiply_reduce_fusion.5 = (f32[48,48,640]{2,1,0:T(8,128)}, f32[48,48,640]{2,1,0:T(8,128)}) fusion(f32[12,2,48,640]{3,2,1,0:T(8,128)} %convert_element_type.155, f32[12,2,48,640]{3,2,1,0:T(8,128)S(1)} %copy-done.3, f32[12,2,48,640]{3,2,1,0:T(8,128)S(1)} %maximum_convert_fusion.1), kind=kLoop, calls=%fused_computation.5 | loop fusion | flops 138608640 | bytes 20643840 | tf_op jit(solution)/shard_map/reduce_sum | solution.py:83
  211.4 7.3 %fusion.17 = bf16[48,48,256]{2,1,0:T(8,128)(2,1)} fusion(bf16[1280,256,1]{1,0,2:T(8,128)(2,1)} %bitcast.228, f32[48,48,640]{2,1,0:T(8,128)} %get-tuple-element.32, f32[48,48,640]{2,1,0:T(8,128)} %get-tuple-element.31), kind=kOutput, calls=%fused_computation.31 | convolution fusion | flops 1519976448 | bytes 13631488 | tf_op jit(solution)/shard_map/dot_general | solution.py:88
  218.7 2.7 fusion.56
  221.4 1.8 maximum_convert_fusion.2
  223.4 1.7 maximum_convert_fusion.3
  225.4 1.6 copy-done.2
  226.9 34.2 %multiply_reduce_fusion.3 = (f32[48,48,640]{2,1,0:T(8,128)}, f32[48,48,640]{2,1,0:T(8,128)}) fusion(f32[12,2,48,640]{3,2,1,0:T(8,128)S(1)} %convert_element_type.160, f32[12,2,48,640]{3,2,1,0:T(8,128)S(1)} %copy-done.2, f32[12,2,48,640]{3,2,1,0:T(8,128)} %maximum_convert_fusion.2), kind=kLoop, calls=%fused_computation.3 | loop fusion | flops 138608640 | bytes 20643840 | tf_op jit(solution)/shard_map/reduce_sum | solution.py:83
  261.2 7.2 %fusion.20 = bf16[48,48,256]{2,1,0:T(8,128)(2,1)} fusion(bf16[1280,256,1]{1,0,2:T(8,128)(2,1)S(1)} %bitcast.229, f32[48,48,640]{2,1,0:T(8,128)} %get-tuple-element.30, f32[48,48,640]{2,1,0:T(8,128)} %get-tuple-element.29), kind=kOutput, calls=%fused_computation.32 | convolution fusion | flops 1519976448 | bytes 13631488 | tf_op jit(solution)/shard_map/dot_general | solution.py:88
  268.6 1.6 copy-done.1
  270.2 34.2 %multiply_reduce_fusion.1 = (f32[48,48,640]{2,1,0:T(8,128)}, f32[48,48,640]{2,1,0:T(8,128)}) fusion(f32[12,2,48,640]{3,2,1,0:T(8,128)S(1)} %convert_element_type.166, f32[12,2,48,640]{3,2,1,0:T(8,128)S(1)} %copy-done.1, f32[12,2,48,640]{3,2,1,0:T(8,128)} %maximum_convert_fusion.3), kind=kLoop, calls=%fused_computation.1 | loop fusion | flops 138608640 | bytes 20643840 | tf_op jit(solution)/shard_map/reduce_sum | solution.py:83
  304.4 7.2 %fusion.23 = bf16[48,48,256]{2,1,0:T(8,128)(2,1)} fusion(bf16[1280,256,1]{1,0,2:T(8,128)(2,1)S(1)} %bitcast.230, f32[48,48,640]{2,1,0:T(8,128)} %get-tuple-element.28, f32[48,48,640]{2,1,0:T(8,128)} %get-tuple-element.27), kind=kOutput, calls=%fused_computation.33 | convolution fusion | flops 1519976448 | bytes 13631488 | tf_op jit(solution)/shard_map/dot_general | solution.py:88
  312.2 21.6 %reduce-scatter.11.cloned.1.call-done = bf16[24,48,256]{2,1,0:T(8,128)(2,1)} async-done(((bf16[48,48,256]{2,1,0:T(8,128)(2,1)}), bf16[24,48,256]{2,1,0:T(8,128)(2,1)}) %reduce-scatter.11.cloned.1.call-update) | async-done | bytes 589840 | tf_op jit(solution)/shard_map/reduce_scatter | solution.py:108
  333.8 27.6 %reduce-scatter.9.cloned.1.call-done = bf16[24,48,256]{2,1,0:T(8,128)(2,1)} async-done(((bf16[48,48,256]{2,1,0:T(8,128)(2,1)}), bf16[24,48,256]{2,1,0:T(8,128)(2,1)}) %reduce-scatter.9.cloned.1.call-update) | async-done | bytes 589840 | tf_op jit(solution)/shard_map/reduce_scatter | solution.py:108
  361.4 2.9 pad_maximum_fusion.1
  (145 shorter events, 15.1 us)
Async XLA Ops:
  6.5 218.6 %reduce-scatter.5.cloned.1.call-start = ((), (), s32[]{:S(2)}) async-start(), calls=%async_computation.4 | async-start | bytes 1769472 | tf_op jit(solution)/shard_map/reduce_scatter | solution.py:108
  18.0 6.1 %copy-start.5 = (bf16[32,48,640]{2,1,0:T(8,128)(2,1)S(1)}, bf16[32,48,640]{2,1,0:T(8,128)(2,1)}, u32[]{:S(2)}) copy-start(bf16[32,48,640]{2,1,0:T(8,128)(2,1)} %get-tuple-element.45) | copy-start | bytes 5898244
  18.1 7.6 %copy-start = (bf16[1,12,2,48,640]{4,3,2,1,0:T(8,128)(2,1)S(1)}, bf16[1,12,2,48,640]{4,3,2,1,0:T(8,128)(2,1)}, u32[]{:S(2)}) copy-start(bf16[1,12,2,48,640]{4,3,2,1,0:T(8,128)(2,1)} %param.3) | copy-start | bytes 4423684
  20.4 10.4 %collective-permute-start.22 = (bf16[2,2,2,2,1,48,640]{6,5,3,2,1,0,4:T(8,128)(2,1)}, bf16[2,2,2,2,1,48,640]{6,5,3,2,1,0,4:T(8,128)(2,1)}, u32[]{:S(2)}, u32[]{:S(2)}) collective-permute-start(bf16[2,2,2,2,1,48,640]{6,5,3,2,1,0,4:T(8,128)(2,1)} %dynamic-slice_bitcast_fusion), channel_id=1, source_target_pairs={{0,2},{2,0},{4,6},{6,4},{8,10},{10,8},{12,14},{14,12},{16,18},{18,... | collective-permute-start | bytes 2949128 | tf_op jit(solution)/shard_map/ppermute | solution.py:21
  24.1 11.1 %collective-permute-start.11 = (bf16[2,2,2,2,1,48,640]{6,5,3,2,1,0,4:T(8,128)(2,1)}, bf16[2,2,2,2,1,48,640]{6,5,3,2,1,0,4:T(8,128)(2,1)}, u32[]{:S(2)}, u32[]{:S(2)}) collective-permute-start(bf16[2,2,2,2,1,48,640]{6,5,3,2,1,0,4:T(8,128)(2,1)} %dynamic-slice_bitcast_fusion.1), channel_id=1, source_target_pairs={{0,2},{2,0},{4,6},{6,4},{8,10},{10,8},{12,14},{14,12},{16,18},{18,... | collective-permute-start | bytes 2949128 | tf_op jit(solution)/shard_map/ppermute | solution.py:21
  25.2 12.9 %collective-permute-start = (bf16[2,2,2,2,1,48,640]{6,5,3,2,1,0,4:T(8,128)(2,1)}, bf16[2,2,2,2,1,48,640]{6,5,3,2,1,0,4:T(8,128)(2,1)}, u32[]{:S(2)}, u32[]{:S(2)}) collective-permute-start(bf16[2,2,2,2,1,48,640]{6,5,3,2,1,0,4:T(8,128)(2,1)} %dynamic-slice_bitcast_fusion.2), channel_id=1, source_target_pairs={{0,2},{2,0},{4,6},{6,4},{8,10},{10,8},{12,14},{14,12},{16,18},{18,... | collective-permute-start | bytes 2949128 | tf_op jit(solution)/shard_map/ppermute | solution.py:21
  25.7 5.2 %copy-start.8 = (bf16[32,48,640]{2,1,0:T(8,128)(2,1)S(1)}, bf16[32,48,640]{2,1,0:T(8,128)(2,1)}, u32[]{:S(2)}) copy-start(bf16[32,48,640]{2,1,0:T(8,128)(2,1)} %get-tuple-element.43) | copy-start | bytes 5898244
  27.8 7.5 %copy-start.7 = (bf16[32,48,640]{2,1,0:T(8,128)(2,1)S(1)}, bf16[32,48,640]{2,1,0:T(8,128)(2,1)}, u32[]{:S(2)}) copy-start(bf16[32,48,640]{2,1,0:T(8,128)(2,1)} %get-tuple-element.44) | copy-start | bytes 5898244
  32.2 5.8 %copy-start.6 = (bf16[32,48,640]{2,1,0:T(8,128)(2,1)S(1)}, bf16[32,48,640]{2,1,0:T(8,128)(2,1)}, u32[]{:S(2)}) copy-start(bf16[32,48,640]{2,1,0:T(8,128)(2,1)} %get-tuple-element.45) | copy-start | bytes 5898244
  32.3 14.3 %collective-permute-start.23 = (bf16[2,2,2,1,48,640]{5,4,2,1,0,3:T(8,128)(2,1)S(1)}, bf16[2,2,2,1,48,640]{5,4,2,1,0,3:T(8,128)(2,1)S(1)}, u32[]{:S(2)}, u32[]{:S(2)}) collective-permute-start(bf16[2,2,2,1,48,640]{5,4,2,1,0,3:T(8,128)(2,1)S(1)} %dynamic-slice_bitcast_fusion.3), channel_id=1, source_target_pairs={{0,64},{2,66},{4,68},{6,70},{8,72},{10,74},{12,76},{14,78},{16,80}... | collective-permute-start | bytes 1474568 | tf_op jit(solution)/shard_map/ppermute | solution.py:21
  36.7 12.6 %collective-permute-start.12 = (bf16[2,2,2,1,48,640]{5,4,2,1,0,3:T(8,128)(2,1)S(1)}, bf16[2,2,2,1,48,640]{5,4,2,1,0,3:T(8,128)(2,1)S(1)}, u32[]{:S(2)}, u32[]{:S(2)}) collective-permute-start(bf16[2,2,2,1,48,640]{5,4,2,1,0,3:T(8,128)(2,1)S(1)} %dynamic-slice_bitcast_fusion.4), channel_id=1, source_target_pairs={{0,16},{2,18},{4,20},{6,22},{8,24},{10,26},{12,28},{14,30},{16,0},... | collective-permute-start | bytes 1474568 | tf_op jit(solution)/shard_map/ppermute | solution.py:21
  39.5 12.6 %collective-permute-start.1 = (bf16[2,2,2,1,48,640]{5,4,2,1,0,3:T(8,128)(2,1)S(1)}, bf16[2,2,2,1,48,640]{5,4,2,1,0,3:T(8,128)(2,1)S(1)}, u32[]{:S(2)}, u32[]{:S(2)}) collective-permute-start(bf16[2,2,2,1,48,640]{5,4,2,1,0,3:T(8,128)(2,1)S(1)} %dynamic-slice_bitcast_fusion.5), channel_id=1, source_target_pairs={{0,4},{2,6},{4,0},{6,2},{8,12},{10,14},{12,8},{14,10},{16,20},{18,... | collective-permute-start | bytes 1474568 | tf_op jit(solution)/shard_map/ppermute | solution.py:21
  46.8 10.6 %collective-permute-start.24 = (bf16[2,2,1,48,640]{4,3,1,2,0:T(8,128)(2,1)S(1)}, bf16[2,2,1,48,640]{4,3,1,2,0:T(8,128)(2,1)S(1)}, u32[]{:S(2)}, u32[]{:S(2)}) collective-permute-start(bf16[2,2,1,48,640]{4,3,1,2,0:T(8,128)(2,1)S(1)} %dynamic-slice_bitcast_fusion.6), channel_id=1, source_target_pairs={{0,4},{2,6},{4,0},{6,2},{8,12},{10,14},{12,8},{14,10},{16,20},{18,... | collective-permute-start | bytes 737288 | tf_op jit(solution)/shard_map/ppermute | solution.py:21
  49.3 8.4 %collective-permute-start.13 = (bf16[2,2,1,48,640]{4,3,1,2,0:T(8,128)(2,1)S(1)}, bf16[2,2,1,48,640]{4,3,1,2,0:T(8,128)(2,1)S(1)}, u32[]{:S(2)}, u32[]{:S(2)}) collective-permute-start(bf16[2,2,1,48,640]{4,3,1,2,0:T(8,128)(2,1)S(1)} %dynamic-slice_bitcast_fusion.7), channel_id=1, source_target_pairs={{0,64},{2,66},{4,68},{6,70},{8,72},{10,74},{12,76},{14,78},{16,80}... | collective-permute-start | bytes 737288 | tf_op jit(solution)/shard_map/ppermute | solution.py:21
  52.2 6.9 %collective-permute-start.2 = (bf16[2,2,1,48,640]{4,3,1,2,0:T(8,128)(2,1)S(1)}, bf16[2,2,1,48,640]{4,3,1,2,0:T(8,128)(2,1)S(1)}, u32[]{:S(2)}, u32[]{:S(2)}) collective-permute-start(bf16[2,2,1,48,640]{4,3,1,2,0:T(8,128)(2,1)S(1)} %dynamic-slice_bitcast_fusion.8), channel_id=1, source_target_pairs={{0,16},{2,18},{4,20},{6,22},{8,24},{10,26},{12,28},{14,30},{16,0},... | collective-permute-start | bytes 737288 | tf_op jit(solution)/shard_map/ppermute | solution.py:21
  57.4 3.8 %collective-permute-start.25 = (bf16[2,1,48,640]{3,2,1,0:T(8,128)(2,1)S(1)}, bf16[2,1,48,640]{3,2,1,0:T(8,128)(2,1)S(1)}, u32[]{:S(2)}, u32[]{:S(2)}) collective-permute-start(bf16[2,1,48,640]{3,2,1,0:T(8,128)(2,1)S(1)} %dynamic-slice_bitcast_fusion.9), channel_id=1, source_target_pairs={{0,16},{2,18},{4,20},{6,22},{8,24},{10,26},{12,28},{14,30},{16,0},... | collective-permute-start | bytes 368648 | tf_op jit(solution)/shard_map/ppermute | solution.py:21
  57.7 7.2 %collective-permute-start.14 = (bf16[2,1,48,640]{3,2,1,0:T(8,128)(2,1)S(1)}, bf16[2,1,48,640]{3,2,1,0:T(8,128)(2,1)S(1)}, u32[]{:S(2)}, u32[]{:S(2)}) collective-permute-start(bf16[2,1,48,640]{3,2,1,0:T(8,128)(2,1)S(1)} %dynamic-slice_bitcast_fusion.10), channel_id=1, source_target_pairs={{0,4},{2,6},{4,0},{6,2},{8,12},{10,14},{12,8},{14,10},{16,20},{18,... | collective-permute-start | bytes 368648 | tf_op jit(solution)/shard_map/ppermute | solution.py:21
  59.2 8.5 %collective-permute-start.3 = (bf16[2,1,48,640]{3,2,1,0:T(8,128)(2,1)S(1)}, bf16[2,1,48,640]{3,2,1,0:T(8,128)(2,1)S(1)}, u32[]{:S(2)}, u32[]{:S(2)}) collective-permute-start(bf16[2,1,48,640]{3,2,1,0:T(8,128)(2,1)S(1)} %dynamic-slice_bitcast_fusion.11), channel_id=1, source_target_pairs={{0,64},{2,66},{4,68},{6,70},{8,72},{10,74},{12,76},{14,78},{16,80}... | collective-permute-start | bytes 368648 | tf_op jit(solution)/shard_map/ppermute | solution.py:21
  61.3 6.9 %collective-permute-start.26 = (bf16[1,48,640]{2,1,0:T(8,128)(2,1)S(1)}, bf16[1,48,640]{2,1,0:T(8,128)(2,1)S(1)}, u32[]{:S(2)}, u32[]{:S(2)}) collective-permute-start(bf16[1,48,640]{2,1,0:T(8,128)(2,1)S(1)} %dynamic-slice_bitcast_fusion.12), channel_id=1, source_target_pairs={{0,8},{2,10},{4,12},{6,14},{8,0},{10,2},{12,4},{14,6},{16,24},{18,... | collective-permute-start | bytes 184328 | tf_op jit(solution)/shard_map/ppermute | solution.py:21
  65.0 5.9 %collective-permute-start.15 = (bf16[1,48,640]{2,1,0:T(8,128)(2,1)S(1)}, bf16[1,48,640]{2,1,0:T(8,128)(2,1)S(1)}, u32[]{:S(2)}, u32[]{:S(2)}) collective-permute-start(bf16[1,48,640]{2,1,0:T(8,128)(2,1)S(1)} %dynamic-slice_bitcast_fusion.13), channel_id=1, source_target_pairs={{0,32},{2,34},{4,36},{6,38},{8,40},{10,42},{12,44},{14,46},{16,48}... | collective-permute-start | bytes 184328 | tf_op jit(solution)/shard_map/ppermute | solution.py:21
  67.7 5.0 %collective-permute-start.4 = (bf16[1,48,640]{2,1,0:T(8,128)(2,1)S(1)}, bf16[1,48,640]{2,1,0:T(8,128)(2,1)S(1)}, u32[]{:S(2)}, u32[]{:S(2)}) collective-permute-start(bf16[1,48,640]{2,1,0:T(8,128)(2,1)S(1)} %dynamic-slice_bitcast_fusion.14), channel_id=1, source_target_pairs={{0,8},{2,10},{4,12},{6,14},{8,0},{10,2},{12,4},{14,6},{16,24},{18,... | collective-permute-start | bytes 184328 | tf_op jit(solution)/shard_map/ppermute | solution.py:21
  68.3 5.8 %collective-permute-start.27 = (bf16[1,48,640]{2,1,0:T(8,128)(2,1)S(1)}, bf16[1,48,640]{2,1,0:T(8,128)(2,1)S(1)}, u32[]{:S(2)}, u32[]{:S(2)}) collective-permute-start(bf16[1,48,640]{2,1,0:T(8,128)(2,1)S(1)} %bitcast_add_fusion.12), channel_id=1, source_target_pairs={{0,32},{2,34},{4,36},{6,38},{8,40},{10,42},{12,44},{14,46},{16,48}... | collective-permute-start | bytes 184328 | tf_op jit(solution)/shard_map/ppermute | solution.py:21
  70.9 5.9 %collective-permute-start.16 = (bf16[1,48,640]{2,1,0:T(8,128)(2,1)S(1)}, bf16[1,48,640]{2,1,0:T(8,128)(2,1)S(1)}, u32[]{:S(2)}, u32[]{:S(2)}) collective-permute-start(bf16[1,48,640]{2,1,0:T(8,128)(2,1)S(1)} %bitcast_add_fusion.13), channel_id=1, source_target_pairs={{0,8},{2,10},{4,12},{6,14},{8,0},{10,2},{12,4},{14,6},{16,24},{18,... | collective-permute-start | bytes 184328 | tf_op jit(solution)/shard_map/ppermute | solution.py:21
  72.7 5.5 %collective-permute-start.5 = (bf16[1,48,640]{2,1,0:T(8,128)(2,1)S(1)}, bf16[1,48,640]{2,1,0:T(8,128)(2,1)S(1)}, u32[]{:S(2)}, u32[]{:S(2)}) collective-permute-start(bf16[1,48,640]{2,1,0:T(8,128)(2,1)S(1)} %bitcast_add_fusion.14), channel_id=1, source_target_pairs={{0,32},{2,34},{4,36},{6,38},{8,40},{10,42},{12,44},{14,46},{16,48}... | collective-permute-start | bytes 184328 | tf_op jit(solution)/shard_map/ppermute | solution.py:21
  74.1 6.3 %collective-permute-start.28 = (bf16[1,48,640]{2,1,0:T(8,128)(2,1)S(1)}, bf16[1,48,640]{2,1,0:T(8,128)(2,1)S(1)}, u32[]{:S(2)}, u32[]{:S(2)}) collective-permute-start(bf16[1,48,640]{2,1,0:T(8,128)(2,1)S(1)} %add.213), channel_id=1, source_target_pairs={{0,8},{2,10},{4,12},{6,14},{8,0},{10,2},{12,4},{14,6},{16,24},{18,... | collective-permute-start | bytes 184328 | tf_op jit(solution)/shard_map/ppermute | solution.py:21
  76.9 5.1 %collective-permute-start.17 = (bf16[1,48,640]{2,1,0:T(8,128)(2,1)S(1)}, bf16[1,48,640]{2,1,0:T(8,128)(2,1)S(1)}, u32[]{:S(2)}, u32[]{:S(2)}) collective-permute-start(bf16[1,48,640]{2,1,0:T(8,128)(2,1)S(1)} %add.203), channel_id=1, source_target_pairs={{0,32},{2,34},{4,36},{6,38},{8,40},{10,42},{12,44},{14,46},{16,48}... | collective-permute-start | bytes 184328 | tf_op jit(solution)/shard_map/ppermute | solution.py:21
  78.2 5.4 %collective-permute-start.6 = (bf16[1,48,640]{2,1,0:T(8,128)(2,1)S(1)}, bf16[1,48,640]{2,1,0:T(8,128)(2,1)S(1)}, u32[]{:S(2)}, u32[]{:S(2)}) collective-permute-start(bf16[1,48,640]{2,1,0:T(8,128)(2,1)S(1)} %add.195), channel_id=1, source_target_pairs={{0,8},{2,10},{4,12},{6,14},{8,0},{10,2},{12,4},{14,6},{16,24},{18,... | collective-permute-start | bytes 184328 | tf_op jit(solution)/shard_map/ppermute | solution.py:21
  80.4 4.4 %collective-permute-start.29 = (bf16[2,1,48,640]{3,2,0,1:T(8,128)(2,1)S(1)}, bf16[2,1,48,640]{3,2,0,1:T(8,128)(2,1)S(1)}, u32[]{:S(2)}, u32[]{:S(2)}) collective-permute-start(bf16[2,1,48,640]{3,2,0,1:T(8,128)(2,1)S(1)} %pad_maximum_fusion.19), channel_id=1, source_target_pairs={{0,16},{2,18},{4,20},{6,22},{8,24},{10,26},{12,28},{14,30},{16,0},... | collective-permute-start | bytes 368648 | tf_op jit(solution)/shard_map/ppermute | solution.py:21
  82.1 4.1 %collective-permute-start.18 = (bf16[2,1,48,640]{3,2,0,1:T(8,128)(2,1)S(1)}, bf16[2,1,48,640]{3,2,0,1:T(8,128)(2,1)S(1)}, u32[]{:S(2)}, u32[]{:S(2)}) collective-permute-start(bf16[2,1,48,640]{3,2,0,1:T(8,128)(2,1)S(1)} %pad_maximum_fusion.18), channel_id=1, source_target_pairs={{0,4},{2,6},{4,0},{6,2},{8,12},{10,14},{12,8},{14,10},{16,20},{18,... | collective-permute-start | bytes 368648 | tf_op jit(solution)/shard_map/ppermute | solution.py:21
  83.6 5.5 %collective-permute-start.7 = (bf16[2,1,48,640]{3,2,0,1:T(8,128)(2,1)S(1)}, bf16[2,1,48,640]{3,2,0,1:T(8,128)(2,1)S(1)}, u32[]{:S(2)}, u32[]{:S(2)}) collective-permute-start(bf16[2,1,48,640]{3,2,0,1:T(8,128)(2,1)S(1)} %fusion.38), channel_id=1, source_target_pairs={{0,64},{2,66},{4,68},{6,70},{8,72},{10,74},{12,76},{14,78},{16,80}... | collective-permute-start | bytes 368648 | tf_op jit(solution)/shard_map/ppermute | solution.py:21
  84.9 5.3 %collective-permute-start.30 = (bf16[2,2,1,48,640]{4,3,1,0,2:T(8,128)(2,1)S(1)}, bf16[2,2,1,48,640]{4,3,1,0,2:T(8,128)(2,1)S(1)}, u32[]{:S(2)}, u32[]{:S(2)}) collective-permute-start(bf16[2,2,1,48,640]{4,3,1,0,2:T(8,128)(2,1)S(1)} %pad_maximum_fusion.16), channel_id=1, source_target_pairs={{0,4},{2,6},{4,0},{6,2},{8,12},{10,14},{12,8},{14,10},{16,20},{18,... | collective-permute-start | bytes 737288 | tf_op jit(solution)/shard_map/ppermute | solution.py:21
  86.2 7.0 %collective-permute-start.19 = (bf16[2,2,1,48,640]{4,3,1,0,2:T(8,128)(2,1)S(1)}, bf16[2,2,1,48,640]{4,3,1,0,2:T(8,128)(2,1)S(1)}, u32[]{:S(2)}, u32[]{:S(2)}) collective-permute-start(bf16[2,2,1,48,640]{4,3,1,0,2:T(8,128)(2,1)S(1)} %pad_maximum_fusion.15), channel_id=1, source_target_pairs={{0,64},{2,66},{4,68},{6,70},{8,72},{10,74},{12,76},{14,78},{16,80}... | collective-permute-start | bytes 737288 | tf_op jit(solution)/shard_map/ppermute | solution.py:21
  89.2 5.4 %collective-permute-start.8 = (bf16[2,2,1,48,640]{4,3,1,0,2:T(8,128)(2,1)S(1)}, bf16[2,2,1,48,640]{4,3,1,0,2:T(8,128)(2,1)S(1)}, u32[]{:S(2)}, u32[]{:S(2)}) collective-permute-start(bf16[2,2,1,48,640]{4,3,1,0,2:T(8,128)(2,1)S(1)} %fusion.36), channel_id=1, source_target_pairs={{0,16},{2,18},{4,20},{6,22},{8,24},{10,26},{12,28},{14,30},{16,0},... | collective-permute-start | bytes 737288 | tf_op jit(solution)/shard_map/ppermute | solution.py:21
  90.3 14.2 %collective-permute-start.31 = (bf16[2,2,2,1,48,640]{5,4,2,1,0,3:T(8,128)(2,1)S(1)}, bf16[2,2,2,1,48,640]{5,4,2,1,0,3:T(8,128)(2,1)S(1)}, u32[]{:S(2)}, u32[]{:S(2)}) collective-permute-start(bf16[2,2,2,1,48,640]{5,4,2,1,0,3:T(8,128)(2,1)S(1)} %pad_maximum_fusion.13), channel_id=1, source_target_pairs={{0,64},{2,66},{4,68},{6,70},{8,72},{10,74},{12,76},{14,78},{16,80}... | collective-permute-start | bytes 1474568 | tf_op jit(solution)/shard_map/ppermute | solution.py:21
  93.4 16.1 %collective-permute-start.20 = (bf16[2,2,2,1,48,640]{5,4,2,1,0,3:T(8,128)(2,1)S(1)}, bf16[2,2,2,1,48,640]{5,4,2,1,0,3:T(8,128)(2,1)S(1)}, u32[]{:S(2)}, u32[]{:S(2)}) collective-permute-start(bf16[2,2,2,1,48,640]{5,4,2,1,0,3:T(8,128)(2,1)S(1)} %pad_maximum_fusion.12), channel_id=1, source_target_pairs={{0,16},{2,18},{4,20},{6,22},{8,24},{10,26},{12,28},{14,30},{16,0},... | collective-permute-start | bytes 1474568 | tf_op jit(solution)/shard_map/ppermute | solution.py:21
  94.8 17.5 %collective-permute-start.9 = (bf16[2,2,2,1,48,640]{5,4,2,1,0,3:T(8,128)(2,1)S(1)}, bf16[2,2,2,1,48,640]{5,4,2,1,0,3:T(8,128)(2,1)S(1)}, u32[]{:S(2)}, u32[]{:S(2)}) collective-permute-start(bf16[2,2,2,1,48,640]{5,4,2,1,0,3:T(8,128)(2,1)S(1)} %fusion.34), channel_id=1, source_target_pairs={{0,4},{2,6},{4,0},{6,2},{8,12},{10,14},{12,8},{14,10},{16,20},{18,... | collective-permute-start | bytes 1474568 | tf_op jit(solution)/shard_map/ppermute | solution.py:21
  104.7 9.2 %collective-permute-start.32 = (bf16[2,2,2,2,1,48,640]{6,5,3,2,1,0,4:T(8,128)(2,1)S(1)}, bf16[2,2,2,2,1,48,640]{6,5,3,2,1,0,4:T(8,128)(2,1)S(1)}, u32[]{:S(2)}, u32[]{:S(2)}) collective-permute-start(bf16[2,2,2,2,1,48,640]{6,5,3,2,1,0,4:T(8,128)(2,1)S(1)} %pad_maximum_fusion.9), channel_id=1, source_target_pairs={{0,2},{2,0},{4,6},{6,4},{8,10},{10,8},{12,14},{14,12},{16,18},{18,... | collective-permute-start | bytes 2949128 | tf_op jit(solution)/shard_map/ppermute | solution.py:21
  109.7 4.2 %copy-start.15 = (s32[2,12]{1,0:T(2,128)S(1)}, s32[2,12]{1,0:T(2,128)}, u32[]{:S(2)}) copy-start(s32[2,12]{1,0:T(2,128)} %param.4) | copy-start | bytes 292
  109.7 4.7 %collective-permute-start.21 = (bf16[2,2,2,2,1,48,640]{6,5,3,2,1,0,4:T(8,128)(2,1)S(1)}, bf16[2,2,2,2,1,48,640]{6,5,3,2,1,0,4:T(8,128)(2,1)S(1)}, u32[]{:S(2)}, u32[]{:S(2)}) collective-permute-start(bf16[2,2,2,2,1,48,640]{6,5,3,2,1,0,4:T(8,128)(2,1)S(1)} %pad_maximum_fusion.8), channel_id=1, source_target_pairs={{0,2},{2,0},{4,6},{6,4},{8,10},{10,8},{12,14},{14,12},{16,18},{18,... | collective-permute-start | bytes 2949128 | tf_op jit(solution)/shard_map/ppermute | solution.py:21
  112.5 3.5 collective-permute-start.10
  127.1 2.9 copy-start.4
  173.3 95.1 %reduce-scatter.7.cloned.1.call-start = ((), (), s32[]{:S(2)}) async-start(), calls=%async_computation.5 | async-start | bytes 1769472 | tf_op jit(solution)/shard_map/reduce_scatter | solution.py:108
  173.5 1.8 copy-start.3
  211.4 7.3 %copy-start.9 = (bf16[12,2,48,640]{3,2,1,0:T(8,128)(2,1)S(1)}, bf16[12,2,48,640]{3,2,1,0:T(8,128)(2,1)}, u32[]{:S(2)}) copy-start(bf16[12,2,48,640]{3,2,1,0:T(8,128)(2,1)} %get-tuple-element.36) | copy-start | bytes 4423684
  221.4 1.9 copy-start.10
  221.4 1.9 copy-start.11
  223.3 110.5 %reduce-scatter.11.cloned.1.call-start = ((), (), s32[]{:S(2)}) async-start(), calls=%async_computation.7 | async-start | bytes 1769472 | tf_op jit(solution)/shard_map/reduce_scatter | solution.py:108
  225.1 1.8 copy-start.2
  226.9 34.2 %copy-start.12 = (bf16[2,640,256]{2,1,0:T(8,128)(2,1)S(1)}, bf16[2,640,256]{2,1,0:T(8,128)(2,1)}, u32[]{:S(2)}) copy-start(bf16[2,640,256]{2,1,0:T(8,128)(2,1)} %pad_maximum_fusion.10) | copy-start | bytes 1966084
  268.3 1.8 copy-start.1
  304.4 57.0 %copy-start.13 = (bf16[24,48,256]{2,1,0:T(8,128)(2,1)S(1)}, bf16[24,48,256]{2,1,0:T(8,128)(2,1)}, u32[]{:S(2)}) copy-start(bf16[24,48,256]{2,1,0:T(8,128)(2,1)} %reduce-scatter.5.cloned.1.call-done) | copy-start | bytes 1769476
  304.4 57.0 %copy-start.14 = (bf16[24,48,256]{2,1,0:T(8,128)(2,1)S(1)}, bf16[24,48,256]{2,1,0:T(8,128)(2,1)}, u32[]{:S(2)}) copy-start(bf16[24,48,256]{2,1,0:T(8,128)(2,1)} %reduce-scatter.7.cloned.1.call-done) | copy-start | bytes 1769476
  311.6 49.7 %reduce-scatter.9.cloned.1.call-start = ((), (), s32[]{:S(2)}) async-start(), calls=%async_computation.6 | async-start | bytes 1769472 | tf_op jit(solution)/shard_map/reduce_scatter | solution.py:108
Sparse Core Ops, SparseCore 0:
  173.4 21.9 reduce-scatter.4
  223.4 21.9 reduce-scatter.6
  311.8 21.9 reduce-scatter.10
  336.0 25.3 reduce-scatter.8
